TPU v7x, 32 devices: a whole 2x2x4 slice. The times are simulated.
32 devices in a mesh: freq: 4 (over x, core), tile: 8 (over z, y).
Axes of the slice: x: 2, y: 2, z: 4, core: 2. Of those that a mesh axis runs over, the one named last changes fastest.
Arguments:
- travel_time: float32 [512, 8, 512], P('tile', None, 'freq'), may hold values from 0 to 4
- crossing: int32 [8, 512], P('tile'), may hold values from 0 to 63
- bins: int32 [4], P('freq'), may hold values from 8 to 71
- transmission: float32 [4, 2, 64], P('freq'), may hold values from -1 to 1
- capture: bfloat16 [4, 2, 512, 512], P('freq', None, 'tile'), may hold values from -0.01171875 to 0.01171875
Outputs:
- image: float32 [2, 8, 512], P(None, 'tile')
All inputs are finite; a program needn't handle non-finite values.
Results may differ from a plain program's by a relative error of at most 0.0033.
Values may be sent and summed in bfloat16 or wider, within the bound.
No kernel may reach another device: no remote copies, remote signals or barrier semaphores. Data moves between devices by JAX's collectives and lax.ppermute only.
A program may use at most 64 MiB of HBM per device.

v0:
```python
import math
import jax
import jax.numpy as jnp
from jax import lax
from jax.sharding import PartitionSpec as P

TWO_PI = 2.0 * math.pi


def make_fields(times, bin_values):
    scaled = (TWO_PI * bin_values.astype(jnp.float32)).reshape((-1,) + (1,) * times.ndim)
    angle = scaled * times[None]
    return jnp.stack(
        [jnp.cos(angle).astype(jnp.bfloat16), (-jnp.sin(angle)).astype(jnp.bfloat16)], axis=1
    )


def body(travel_time, crossing, bins, transmission, capture):
    group = 1
    senders = lax.axis_size("freq")
    sub = lax.axis_index("freq") % group
    regrouped = lax.all_to_all(travel_time, "tile", split_axis=1, concat_axis=0, tiled=True)
    tile_view = lax.all_gather(regrouped, "freq", axis=2, tiled=True)
    fields = make_fields(tile_view, bins)
    count = fields.shape[0]
    elements = fields.shape[2]
    voxels = fields.shape[3] * fields.shape[4]
    flat = fields.reshape(count, 2, elements, voxels)
    stacked = flat.reshape(count, 2 * elements, voxels)
    piece = lax.all_gather(capture, "tile", axis=2, tiled=True)
    rows = piece.shape[2]
    cap_real = piece[0, 0]
    cap_imag = piece[0, 1]
    block = jnp.concatenate(
        [
            jnp.concatenate([cap_real, -cap_imag], axis=1),
            jnp.concatenate([cap_imag, cap_real], axis=1),
        ],
        axis=0,
    )
    product = jnp.dot(block, stacked[0], preferred_element_type=jnp.float32)
    w_real = product[:rows]
    w_imag = product[rows:]
    g_real = flat[0, 0].astype(jnp.float32)
    g_imag = flat[0, 1].astype(jnp.float32)
    sums_real = [jnp.sum(g_real * w_real - g_imag * w_imag, axis=0)]
    sums_imag = [jnp.sum(g_real * w_imag + g_imag * w_real, axis=0)]
    focus_real = jnp.stack(sums_real)
    focus_imag = jnp.stack(sums_imag)
    row_count = crossing.shape[0]
    columns = crossing.shape[1]
    width = columns // (senders * group)
    cross_view = crossing.reshape(row_count, senders, group, width)
    flat_cross = lax.dynamic_index_in_dim(cross_view, sub, 2, keepdims=False).reshape(-1)
    cells = transmission.shape[2]
    match = flat_cross[None, :] == lax.broadcasted_iota(jnp.int32, (cells, 1), 0)
    coeff_real = jnp.sum(
        jnp.where(match[None], transmission[:, 0][:, :, None], jnp.float32(0.0)), axis=1
    )
    coeff_imag = jnp.sum(
        jnp.where(match[None], transmission[:, 1][:, :, None], jnp.float32(0.0)), axis=1
    )
    square_real = coeff_real * coeff_real - coeff_imag * coeff_imag
    square_imag = 2.0 * coeff_real * coeff_imag
    part_real = jnp.sum(square_real * focus_real - square_imag * focus_imag, axis=0)
    part_imag = jnp.sum(square_real * focus_imag + square_imag * focus_real, axis=0)
    local_part = jnp.stack([part_real, part_imag]).reshape(2, row_count, senders, 1, width)
    selector = (lax.broadcasted_iota(jnp.int32, (1, 1, 1, group, 1), 3) == sub).astype(jnp.float32)
    partial_image = (local_part * selector).reshape(2, row_count, columns)
    image = lax.psum(partial_image, "freq")
    return image


def solution(mesh):
    in_specs = (
        P("tile", None, "freq"),
        P("tile", None),
        P("freq"),
        P("freq", None, None),
        P("freq", None, "tile", None),
    )
    out_specs = P(None, "tile", None)
    return jax.shard_map(body, mesh=mesh, in_specs=in_specs, out_specs=out_specs, check_vma=False)
```

profile of v0, /device:TPU:0, one launch (start us, length us, event | category | flops | bytes accessed | tf_op | source)
XLA Modules:
  0.0 89.6 jit_solution(9563920641388800474)
XLA Ops:
  6.5 0.0 all-gather.5.cloned.1.call-start
  6.5 0.7 all-gather.5.cloned.1.call-update
  7.3 0.0 all-gather.3.cloned.1.call-start
  7.3 1.0 %copy.10 = f32[64,8,128]{2,0,1:T(8,128)S(1)} copy(f32[64,8,128]{2,1,0:T(8,128)} %param.5) | data formatting | bytes 524288 | tf_op args[0]
  8.3 17.1 %all_to_all.18 = f32[64,8,128]{2,0,1:T(8,128)} all-to-all(f32[64,8,128]{2,0,1:T(8,128)S(1)} %copy.10), channel_id=1, replica_groups=mesh['freq'=4,'tile'=8] {'tile'}, dimensions={1} | all-to-all | bytes 524288 | tf_op jit(solution)/shard_map/all_to_all | solution.py:22
  25.4 0.0 all-gather.3.cloned.1.call-update
  26.1 0.8 slice_bitcast_fusion.4
  26.8 0.8 select_reduce_fusion.1
  27.6 24.9 %all-gather.5.cloned.1.call-done = bf16[1,2,512,512]{3,2,1,0:T(8,128)(2,1)} async-done(((bf16[1,2,64,512]{3,2,1,0:T(8,128)(2,1)}), bf16[1,2,512,512]{3,2,1,0:T(8,128)(2,1)}) %all-gather.5.cloned.1.call-update) | async-done | bytes 1048592 | tf_op jit(solution)/shard_map/all_gather | solution.py:30
  52.6 1.1 %fusion.15 = bf16[512,512]{1,0:T(8,128)(2,1)S(1)} fusion(bf16[1,2,512,512]{3,2,1,0:T(8,128)(2,1)} %all-gather.5.cloned.1.call-done), kind=kLoop, calls=%fused_computation.36 | loop fusion | flops 262144 | bytes 1048576 | tf_op jit(solution)/shard_map/neg | solution.py:36
  53.7 1.3 %slice_bitcast_fusion.1 = (bf16[512,512]{1,0:T(8,128)(2,1)S(1)}, bf16[512,512]{1,0:T(8,128)(2,1)S(1)}) fusion(bf16[1,2,512,512]{3,2,1,0:T(8,128)(2,1)} %all-gather.5.cloned.1.call-done), kind=kLoop, calls=%fused_computation.22 | loop fusion | bytes 2097152 | tf_op jit(solution)/shard_map/squeeze | solution.py:33
  54.9 14.8 %all-gather.3.cloned.1.call-done = f32[512,1,512]{2,0,1:T(8,128)} async-done(((f32[512,1,128]{2,0,1:T(8,128)}), f32[512,1,512]{2,0,1:T(8,128)}) %all-gather.3.cloned.1.call-update) | async-done | bytes 1048592 | tf_op jit(solution)/shard_map/all_gather | solution.py:23
  69.7 4.7 %fusion.12 = (bf16[1,1,512,1,512]{4,2,1,3,0:T(8,128)(2,1)S(1)}, bf16[1,1,512,1,512]{4,2,1,3,0:T(8,128)(2,1)S(1)}) fusion(f32[512,1,512]{2,0,1:T(8,128)} %all-gather.3.cloned.1.call-done, f32[]{:T(128)} %bitcast.3), kind=kLoop, calls=%fused_computation.19 | loop fusion | flops 1048576 | bytes 2097156 | tf_op jit(solution)/shard_map/convert_element_type | solution.py:14
  74.5 0.1 fusion.16
  74.6 1.2 %fusion = f32[1024,512]{1,0:T(8,128)S(1)} fusion(bf16[1024,512]{1,0:T(8,128)(2,1)S(1)} %bitcast.43, bf16[512,512]{1,0:T(8,128)(2,1)S(1)} %get-tuple-element.12, bf16[512,512]{1,0:T(8,128)(2,1)S(1)} %get-tuple-element.11, bf16[512,512]{1,0:T(8,128)(2,1)S(1)} %fusion.15), kind=kOutput, calls=%fused_computation | convolution fusion | flops 1082130432 | bytes 4718592 | tf_op jit(solution)/shard_map/dot_general | solution.py:41
  75.9 0.4 fusion.11
  76.3 6.5 %psum.7 = f32[2,1,512]{2,1,0:T(1,128)} all-reduce(f32[2,1,512]{2,1,0:T(1,128)S(1)} %pad_maximum_fusion.1), channel_id=1, replica_groups=mesh['freq'=4,'tile'=8] {'freq'}, use_global_device_ids=true, to_apply=%region_4.5 | all-reduce | flops 1024 | bytes 8192 | tf_op jit(solution)/shard_map/psum | solution.py:70
  (2 shorter events, 0.0 us)
Async XLA Ops:
  6.5 46.0 %all-gather.5.cloned.1.call-start = ((), (), s32[]{:S(2)}) async-start(), calls=%async_computation.2 | async-start | bytes 1179648 | tf_op jit(solution)/shard_map/all_gather | solution.py:30
  7.3 62.5 %all-gather.3.cloned.1.call-start = ((), (), s32[]{:S(2)}) async-start(), calls=%async_computation.1 | async-start | bytes 1310720 | tf_op jit(solution)/shard_map/all_gather | solution.py:23
Sparse Core Ops, SparseCore 0:
  9.5 42.9 all-gather.4
  54.1 15.5 all-gather.2
where the time goes:
time: 90 us; the launch traced here: 89.6 us
  waiting for transfers between devices  40.5 us (45%)
  blocking collectives  23.6 us (26%)
  between operations  14.1 us (16%)
  other arithmetic  7.14 us (8%)
  local copies, waits for them, and re-layouts  3.03 us (3%)
  matrix products  1.24 us (1%)
    all_gather x1, waiting for transfers between devices, body(): piece = lax.all_gather(capture, 'tile', axis=2, tiled=True)  24.9 us
    all_to_all x1, blocking collectives, body(): lax.all_to_all(travel_time, 'tile', split_axis=1, concat_axis=0, tiled=True)  17.1 us
    all_gather x1, waiting for transfers between devices, body(): tile_view = lax.all_gather(regrouped, 'freq', axis=2, tiled=True)  14.8 us
    psum x1, blocking collectives, body(): image = lax.psum(partial_image, 'freq')  6.49 us
    convert_element_type x1, other arithmetic, make_fields(): jnp.cos(angle).astype(jnp.bfloat16)  4.75 us
  transfers between devices with their start and end apart: 2, of which 2 were waited for; matrix products, arithmetic and copies ran while one was open for 5% of the time, Pallas kernels for 0%

commit v1 on v0

--- a/solution.py
+++ b/solution.py
@@ -3,6 +3,7 @@
 import jax.numpy as jnp
 from jax import lax
 from jax.sharding import PartitionSpec as P
+from jax.lax import axis_index, axis_size, ppermute
 
 TWO_PI = 2.0 * math.pi
 
@@ -19,7 +20,20 @@
     group = 1
     senders = lax.axis_size("freq")
     sub = lax.axis_index("freq") % group
-    regrouped = lax.all_to_all(travel_time, "tile", split_axis=1, concat_axis=0, tiled=True)
+    before, tmp = (axis_size("tile"), axis_index("tile"))
+    step_out = travel_time.shape[1] // before
+    mixed_arr = list(travel_time.shape)
+    mixed_arr[1] = step_out
+    new = mixed_arr[0]
+    mixed_arr[0] = new * before
+    regrouped = jnp.zeros(mixed_arr, travel_time.dtype)
+    for no in range(before):
+        a_next = lax.dynamic_slice_in_dim(travel_time, (tmp ^ no) * step_out, step_out, axis=1)
+        if no:
+            a_next = ppermute(
+                a_next, axis_name="tile", perm=[(dev, dev ^ no) for dev in range(before)]
+            )
+        regrouped = lax.dynamic_update_slice_in_dim(regrouped, a_next, (tmp ^ no) * new, axis=0)
     tile_view = lax.all_gather(regrouped, "freq", axis=2, tiled=True)
     fields = make_fields(tile_view, bins)
     count = fields.shape[0]

time: 90 us -> 102 us (1.13)
  blocking collectives: 23.6 us -> 6.26 us
  waiting for transfers between devices: 40.5 us -> 56.1 us
  starting transfers between devices: 0.04 us -> 12.7 us
  local copies, waits for them, and re-layouts: 3.03 us -> 5.41 us
  other arithmetic: 7.14 us -> 6.1 us
    all_to_all x1 -> x0, blocking collectives: 17.1 us -> none  [body(): lax.all_to_all(travel_time, 'tile', split_axis=1, concat_axis=0, tiled=True)]
    ppermute x0 -> x7, starting transfers between devices: none -> 12.6 us  [body(): ppermute(a_next, axis_name='tile', perm=[(dev, dev ^ no) for dev in range...]
    all_gather x1, waiting for transfers between devices: 24.9 us -> 37.5 us  [body(): piece = lax.all_gather(capture, 'tile', axis=2, tiled=True)]
    ppermute x0 -> x7, waiting for transfers between devices: none -> 6.52 us  [body(): ppermute(a_next, axis_name='tile', perm=[(dev, dev ^ no) for dev in range...]
    all_gather x1, waiting for transfers between devices: 14.8 us -> 11.3 us  [body(): tile_view = lax.all_gather(regrouped, 'freq', axis=2, tiled=True)]
    dynamic_slice x0 -> x1, local copies, waits for them, and re-layouts: none -> 2.33 us  [body(): lax.dynamic_slice_in_dim(travel_time, (tmp ^ no) * step_out, step_out, ax...]
    neg x1, other arithmetic: 1.08 us -> 0.04 us  [body(): -cap_imag]
  transfers between devices with their start and end apart: 2 -> 9, of which waited for: 2 -> 5; matrix products, arithmetic and copies ran while one was open for 5% -> 6% of each run, Pallas kernels for 0% -> 0%
where the time goes in v1:
time: 102 us
  waiting for transfers between devices  56.1 us (55%)
  between operations  14.2 us (14%)
  starting transfers between devices  12.7 us (12%)
  blocking collectives  6.26 us (6%)
  other arithmetic  6.1 us (6%)
  local copies, waits for them, and re-layouts  5.41 us (5%)
  matrix products  1.24 us (1%)
    all_gather x1, waiting for transfers between devices, body(): piece = lax.all_gather(capture, 'tile', axis=2, tiled=True)  37.5 us
    ppermute x7, starting transfers between devices, body(): ppermute(a_next, axis_name='tile', perm=[(dev, dev ^ no) for dev in range...  12.6 us
    all_gather x1, waiting for transfers between devices, body(): tile_view = lax.all_gather(regrouped, 'freq', axis=2, tiled=True)  11.3 us
    ppermute x7, waiting for transfers between devices, body(): ppermute(a_next, axis_name='tile', perm=[(dev, dev ^ no) for dev in range...  6.52 us
    psum x1, blocking collectives, body(): image = lax.psum(partial_image, 'freq')  6.26 us
    convert_element_type x1, other arithmetic, make_fields(): jnp.cos(angle).astype(jnp.bfloat16)  4.75 us
    dynamic_slice x1, local copies, waits for them, and re-layouts, body(): lax.dynamic_slice_in_dim(travel_time, (tmp ^ no) * step_out, step_out, ax...  2.33 us
  transfers between devices with their start and end apart: 9, of which 5 were waited for; matrix products, arithmetic and copies ran while one was open for 6% of the time, Pallas kernels for 0%

profile of v1, /device:TPU:0, one launch (start us, length us, event | category | flops | bytes accessed | tf_op | source)
XLA Modules:
  0.0 102.0 jit_solution(10711877816600140733)
XLA Ops:
  6.5 0.0 all-gather.3.cloned.1.call-start
  6.5 2.3 %constant_dynamic-slice_fusion = (f32[64,1,128]{2,1,0:T(1,128)S(1)}, f32[64,1,128]{2,1,0:T(1,128)S(1)}, f32[64,1,128]{2,1,0:T(1,128)S(1)}, f32[64,1,128]{2,1,0:T...) fusion(f32[64,8,128]{2,1,0:T(8,128)} %param.5, ...), kind=kLoop, calls=%fused_computation.30 | loop fusion | bytes 524320 | tf_op jit(solution)/shard_map/dynamic_slice | solution.py:31
  8.9 3.0 %collective-permute-start = (f32[64,1,128]{2,0,1:T(8,128)S(1)}, f32[64,1,128]{2,0,1:T(8,128)S(1)}, u32[]{:S(2)}, u32[]{:S(2)}) collective-permute-start(f32[64,1,128]{2,0,1:T(8,128)S(1)} %bitcast.54), channel_id=1, source_target_pairs={{0,1},{1,0},{2,3},{3,2},{4,5},{5,4},{6,7},{7,6},{8,9},{9,8},{10,11... | collective-permute-start | bytes 98312 | tf_op jit(solution)/shard_map/ppermute | solution.py:33
  11.9 1.6 %collective-permute-start.1 = (f32[64,1,128]{2,0,1:T(8,128)S(1)}, f32[64,1,128]{2,0,1:T(8,128)S(1)}, u32[]{:S(2)}, u32[]{:S(2)}) collective-permute-start(f32[64,1,128]{2,0,1:T(8,128)S(1)} %bitcast.53), channel_id=1, source_target_pairs={{0,2},{1,3},{2,0},{3,1},{4,6},{5,7},{6,4},{7,5},{8,10},{9,11},{10,... | collective-permute-start | bytes 98312 | tf_op jit(solution)/shard_map/ppermute | solution.py:33
  13.5 0.0 collective-permute-start.2
  13.5 3.0 %collective-permute-start.3 = (f32[64,1,128]{2,0,1:T(8,128)S(1)}, f32[64,1,128]{2,0,1:T(8,128)S(1)}, u32[]{:S(2)}, u32[]{:S(2)}) collective-permute-start(f32[64,1,128]{2,0,1:T(8,128)S(1)} %bitcast.51), channel_id=1, source_target_pairs={{0,4},{1,5},{2,6},{3,7},{4,0},{5,1},{6,2},{7,3},{8,12},{9,13},{10,... | collective-permute-start | bytes 98312 | tf_op jit(solution)/shard_map/ppermute | solution.py:33
  16.5 1.3 %collective-permute-start.4 = (f32[64,1,128]{2,0,1:T(8,128)S(1)}, f32[64,1,128]{2,0,1:T(8,128)S(1)}, u32[]{:S(2)}, u32[]{:S(2)}) collective-permute-start(f32[64,1,128]{2,0,1:T(8,128)S(1)} %bitcast.50), channel_id=1, source_target_pairs={{0,5},{1,4},{2,7},{3,6},{4,1},{5,0},{6,3},{7,2},{8,13},{9,12},{10,... | collective-permute-start | bytes 98312 | tf_op jit(solution)/shard_map/ppermute | solution.py:33
  17.9 0.0 collective-permute-done
  17.9 3.7 %collective-permute-start.5 = (f32[64,1,128]{2,0,1:T(8,128)S(1)}, f32[64,1,128]{2,0,1:T(8,128)S(1)}, u32[]{:S(2)}, u32[]{:S(2)}) collective-permute-start(f32[64,1,128]{2,0,1:T(8,128)S(1)} %bitcast.49), channel_id=1, source_target_pairs={{0,6},{1,7},{2,4},{3,5},{4,2},{5,3},{6,0},{7,1},{8,14},{9,15},{10,... | collective-permute-start | bytes 98312 | tf_op jit(solution)/shard_map/ppermute | solution.py:33
  21.5 0.0 collective-permute-done.1
  21.5 0.1 collective-permute-start.6
  21.6 0.0 collective-permute-done.2
  21.7 0.0 collective-permute-done.3
  21.7 0.5 collective-permute-done.4
  22.2 1.5 %collective-permute-done.5 = f32[64,1,128]{2,0,1:T(8,128)S(1)} collective-permute-done((f32[64,1,128]{2,0,1:T(8,128)S(1)}, f32[64,1,128]{2,0,1:T(8,128)S(1)}, u32[]{:S(2)}, u32[]{:S(2)}) %collective-permute-start.5) | collective-permute-done | bytes 32800 | tf_op jit(solution)/shard_map/ppermute | solution.py:33
  23.7 4.6 %collective-permute-done.6 = f32[64,1,128]{2,0,1:T(8,128)S(1)} collective-permute-done((f32[64,1,128]{2,0,1:T(8,128)S(1)}, f32[64,1,128]{2,0,1:T(8,128)S(1)}, u32[]{:S(2)}, u32[]{:S(2)}) %collective-permute-start.6) | collective-permute-done | bytes 32800 | tf_op jit(solution)/shard_map/ppermute | solution.py:33
  28.2 0.0 copy-start.1
  28.2 0.7 copy-done.1
  28.9 0.0 all-gather.3.cloned.1.call-update
  28.9 0.0 all-gather.5.cloned.1.call-start
  29.0 0.7 all-gather.5.cloned.1.call-update
  30.4 0.8 slice_bitcast_fusion.4
  31.1 0.8 select_reduce_fusion.1
  31.9 11.3 %all-gather.3.cloned.1.call-done = f32[512,1,512]{2,0,1:T(8,128)} async-done(((f32[512,1,128]{2,0,1:T(8,128)}), f32[512,1,512]{2,0,1:T(8,128)}) %all-gather.3.cloned.1.call-update) | async-done | bytes 1048592 | tf_op jit(solution)/shard_map/all_gather | solution.py:37
  43.2 4.7 %fusion.12 = (bf16[1,1,512,1,512]{4,2,1,3,0:T(8,128)(2,1)S(1)}, bf16[1,1,512,1,512]{4,2,1,3,0:T(8,128)(2,1)S(1)}) fusion(f32[512,1,512]{2,0,1:T(8,128)} %all-gather.3.cloned.1.call-done, f32[]{:T(128)} %bitcast.3), kind=kLoop, calls=%fused_computation.19 | loop fusion | flops 1048576 | bytes 2097156 | tf_op jit(solution)/shard_map/convert_element_type | solution.py:15
  48.0 0.1 fusion.16
  48.1 37.5 %all-gather.5.cloned.1.call-done = bf16[1,2,512,512]{3,2,1,0:T(8,128)(2,1)} async-done(((bf16[1,2,64,512]{3,2,1,0:T(8,128)(2,1)}), bf16[1,2,512,512]{3,2,1,0:T(8,128)(2,1)}) %all-gather.5.cloned.1.call-update) | async-done | bytes 1048592 | tf_op jit(solution)/shard_map/all_gather | solution.py:44
  85.6 0.0 copy-start
  85.6 1.4 %slice_bitcast_fusion.1 = (bf16[512,512]{1,0:T(8,128)(2,1)S(1)}, bf16[512,512]{1,0:T(8,128)(2,1)S(1)}) fusion(bf16[1,2,512,512]{3,2,1,0:T(8,128)(2,1)} %all-gather.5.cloned.1.call-done), kind=kLoop, calls=%fused_computation.22 | loop fusion | bytes 2097152 | tf_op jit(solution)/shard_map/squeeze | solution.py:47
  87.0 0.2 copy-done
  87.2 1.2 %fusion = f32[1024,512]{1,0:T(8,128)S(1)} fusion(bf16[1024,512]{1,0:T(8,128)(2,1)S(1)} %bitcast.46, bf16[512,512]{1,0:T(8,128)(2,1)S(1)} %get-tuple-element.12, bf16[512,512]{1,0:T(8,128)(2,1)S(1)} %get-tuple-element.11, bf16[512,512]{1,0:T(8,128)(2,1)S(1)} %fusion.15), kind=kOutput, calls=%fused_computation | convolution fusion | flops 1082130432 | bytes 4718592 | tf_op jit(solution)/shard_map/dot_general | solution.py:55
  88.4 0.4 fusion.11
  88.9 6.3 %psum.7 = f32[2,1,512]{2,1,0:T(1,128)} all-reduce(f32[2,1,512]{2,1,0:T(1,128)S(1)} %pad_maximum_fusion.1), channel_id=1, replica_groups=mesh['freq'=4,'tile'=8] {'freq'}, use_global_device_ids=true, to_apply=%region_4.5 | all-reduce | flops 1024 | bytes 8192 | tf_op jit(solution)/shard_map/psum | solution.py:84
  (12 shorter events, 0.1 us)
Async XLA Ops:
  6.5 36.7 %all-gather.3.cloned.1.call-start = ((), (), s32[]{:S(2)}) async-start(), calls=%async_computation | async-start | bytes 1310720 | tf_op jit(solution)/shard_map/all_gather | solution.py:37
  8.9 9.0 %collective-permute-start = (f32[64,1,128]{2,0,1:T(8,128)S(1)}, f32[64,1,128]{2,0,1:T(8,128)S(1)}, u32[]{:S(2)}, u32[]{:S(2)}) collective-permute-start(f32[64,1,128]{2,0,1:T(8,128)S(1)} %bitcast.54), channel_id=1, source_target_pairs={{0,1},{1,0},{2,3},{3,2},{4,5},{5,4},{6,7},{7,6},{8,9},{9,8},{10,11... | collective-permute-start | bytes 98312 | tf_op jit(solution)/shard_map/ppermute | solution.py:33
  11.9 9.6 %collective-permute-start.1 = (f32[64,1,128]{2,0,1:T(8,128)S(1)}, f32[64,1,128]{2,0,1:T(8,128)S(1)}, u32[]{:S(2)}, u32[]{:S(2)}) collective-permute-start(f32[64,1,128]{2,0,1:T(8,128)S(1)} %bitcast.53), channel_id=1, source_target_pairs={{0,2},{1,3},{2,0},{3,1},{4,6},{5,7},{6,4},{7,5},{8,10},{9,11},{10,... | collective-permute-start | bytes 98312 | tf_op jit(solution)/shard_map/ppermute | solution.py:33
  13.5 8.2 %collective-permute-start.2 = (f32[64,1,128]{2,0,1:T(8,128)S(1)}, f32[64,1,128]{2,0,1:T(8,128)S(1)}, u32[]{:S(2)}, u32[]{:S(2)}) collective-permute-start(f32[64,1,128]{2,0,1:T(8,128)S(1)} %bitcast.52), channel_id=1, source_target_pairs={{0,3},{1,2},{2,1},{3,0},{4,7},{5,6},{6,5},{7,4},{8,11},{9,10},{10,... | collective-permute-start | bytes 98312 | tf_op jit(solution)/shard_map/ppermute | solution.py:33
  13.5 8.2 %collective-permute-start.3 = (f32[64,1,128]{2,0,1:T(8,128)S(1)}, f32[64,1,128]{2,0,1:T(8,128)S(1)}, u32[]{:S(2)}, u32[]{:S(2)}) collective-permute-start(f32[64,1,128]{2,0,1:T(8,128)S(1)} %bitcast.51), channel_id=1, source_target_pairs={{0,4},{1,5},{2,6},{3,7},{4,0},{5,1},{6,2},{7,3},{8,12},{9,13},{10,... | collective-permute-start | bytes 98312 | tf_op jit(solution)/shard_map/ppermute | solution.py:33
  16.5 5.7 %collective-permute-start.4 = (f32[64,1,128]{2,0,1:T(8,128)S(1)}, f32[64,1,128]{2,0,1:T(8,128)S(1)}, u32[]{:S(2)}, u32[]{:S(2)}) collective-permute-start(f32[64,1,128]{2,0,1:T(8,128)S(1)} %bitcast.50), channel_id=1, source_target_pairs={{0,5},{1,4},{2,7},{3,6},{4,1},{5,0},{6,3},{7,2},{8,13},{9,12},{10,... | collective-permute-start | bytes 98312 | tf_op jit(solution)/shard_map/ppermute | solution.py:33
  17.9 5.8 %collective-permute-start.5 = (f32[64,1,128]{2,0,1:T(8,128)S(1)}, f32[64,1,128]{2,0,1:T(8,128)S(1)}, u32[]{:S(2)}, u32[]{:S(2)}) collective-permute-start(f32[64,1,128]{2,0,1:T(8,128)S(1)} %bitcast.49), channel_id=1, source_target_pairs={{0,6},{1,7},{2,4},{3,5},{4,2},{5,3},{6,0},{7,1},{8,14},{9,15},{10,... | collective-permute-start | bytes 98312 | tf_op jit(solution)/shard_map/ppermute | solution.py:33
  21.5 6.7 %collective-permute-start.6 = (f32[64,1,128]{2,0,1:T(8,128)S(1)}, f32[64,1,128]{2,0,1:T(8,128)S(1)}, u32[]{:S(2)}, u32[]{:S(2)}) collective-permute-start(f32[64,1,128]{2,0,1:T(8,128)S(1)} %bitcast.48), channel_id=1, source_target_pairs={{0,7},{1,6},{2,5},{3,4},{4,3},{5,2},{6,1},{7,0},{8,15},{9,14},{10,... | collective-permute-start | bytes 98312 | tf_op jit(solution)/shard_map/ppermute | solution.py:33
  28.2 0.7 copy-start.1
  28.9 56.7 %all-gather.5.cloned.1.call-start = ((), (), s32[]{:S(2)}) async-start(), calls=%async_computation.1 | async-start | bytes 1179648 | tf_op jit(solution)/shard_map/all_gather | solution.py:44
  85.6 1.5 %copy-start = (bf16[1,2,512,512]{3,2,1,0:T(8,128)(2,1)S(1)}, bf16[1,2,512,512]{3,2,1,0:T(8,128)(2,1)}, u32[]{:S(2)}) copy-start(bf16[1,2,512,512]{3,2,1,0:T(8,128)(2,1)} %all-gather.5.cloned.1.call-done) | copy-start | bytes 3145732
Sparse Core Ops, SparseCore 0:
  29.1 14.0 all-gather.2
  45.4 40.1 all-gather.4
